TPU v7x, 512 devices: a whole 4x4x16 slice. The times are simulated.
512 devices in a mesh: dp: 32 (over z, core), cent: 16 (over y, x).
Axes of the slice: x: 4, y: 4, z: 16, core: 2. Of those that a mesh axis runs over, the one named last changes fastest.
Arguments:
- points: bfloat16 [131072, 1024], P(('dp', 'cent')), may hold values from -22 to 22, as said below
- block_list: int32 [4096, 3], P(('dp', 'cent')), may hold values from 0 to 15, all different within a row; in each aligned block of 8 rows (0 to 7, 8 to 15, ...) at most 2 rows name the same one
- list_count: int32 [4096], P(('dp', 'cent')), may hold values from 1 to 3
- centroids: bfloat16 [16, 1024, 1024], P('cent', 'dp'), may hold values from -14 to 14, as said below
Outputs:
- new_centroids: float32 [16, 1024, 1024], P('cent', 'dp')
Inputs may be any that keep to these rules, and one draw needn't show every extreme that they name: `block_list`: within the rows of one device (aligned blocks of 8 rows) no block id appears more than 2 times, and the ids of one row differ. Only the first list_count[t] entries of row t of block_list are valid. `points`: Real-valued embeddings. Real-valued centroids.
All inputs are finite; a program needn't handle non-finite values.
Results may differ from a plain program's by a relative error of at most 0.0019.
Values may be sent and summed in bfloat16 or wider, within the bound.
No kernel may reach another device: no remote copies, remote signals or barrier semaphores. Data moves between devices by JAX's collectives and lax.ppermute only.
A program may use at most 64 MiB of HBM per device.

v0:
```python
import math
import jax
import jax.numpy as jnp
from jax import lax
from jax.sharding import PartitionSpec as P

score_scale = 2.0
prior_weight = 1.0


def combine_norms(peaks, totals, usable):
    keep = usable[..., None]
    highest = jnp.max(jnp.where(keep, peaks, -1e30), axis=-2)
    summed = jnp.sum(jnp.where(keep, totals * jnp.exp(peaks - highest[..., None, :]), 0.0), axis=-2)
    return highest + jnp.log(summed)


def per_device(points, block_list, list_count, centroids):
    owners = lax.axis_size("cent")
    tiles_here, listed = block_list.shape
    width = points.shape[1]
    tile_rows = points.shape[0] // tiles_here
    capacity = (tiles_here * listed + owners - 1) // owners
    slot_rows = capacity * tile_rows
    scale = score_scale / math.sqrt(width)
    usable = jnp.arange(listed, dtype=jnp.int32)[None, :] < list_count[:, None]
    naming = jnp.logical_and(
        block_list[:, :, None] == jnp.arange(owners, dtype=jnp.int32)[None, None, :],
        usable[:, :, None],
    )
    listing = jnp.any(naming, axis=1).astype(jnp.int32)
    earlier = jnp.cumsum(listing, axis=0) - listing
    placing = jnp.logical_and(
        listing.T[:, None, :] == 1,
        earlier.T[:, None, :] == jnp.arange(capacity, dtype=jnp.int32)[None, :, None],
    )
    placing = placing.astype(jnp.float32).reshape(owners * capacity, tiles_here)
    slot_rank = jnp.take_along_axis(earlier, block_list, axis=1)
    route_code = jnp.where(usable, block_list * capacity + slot_rank, -1)
    outgoing = jnp.dot(
        placing.astype(jnp.bfloat16),
        points.reshape(tiles_here, tile_rows * width),
        preferred_element_type=jnp.float32,
    )
    outgoing = outgoing.astype(jnp.bfloat16).reshape(owners, slot_rows, width)
    slot_routes = (
        jnp.dot(placing, (route_code + 1).astype(jnp.float32), precision=lax.Precision.HIGHEST)
        - 1.0
    )
    slot_routes = slot_routes.astype(jnp.bfloat16).reshape(owners, capacity, listed)
    arrived, arrived_routes = (
        lax.all_to_all(outgoing, "cent", split_axis=0, concat_axis=0, tiled=True),
        lax.all_to_all(slot_routes, "cent", split_axis=0, concat_axis=0, tiled=True),
    )
    incoming = arrived.reshape(owners * slot_rows, width)
    occupied = arrived_routes[:, :, 0] >= 0
    occupied_rows = jnp.broadcast_to(occupied[:, :, None], (owners, capacity, tile_rows)).reshape(
        -1
    )
    logits = (
        lax.dot_general(
            incoming,
            lax.all_gather(centroids, "dp", axis=1, tiled=True)[0],
            (((1,), (1,)), ((), ())),
            preferred_element_type=jnp.float32,
        )
        * scale
    )
    peaks = jnp.max(logits, axis=1)
    totals = jnp.sum(jnp.exp(logits - peaks[:, None]), axis=1)
    back_peaks, back_totals = (
        lax.all_to_all(
            peaks.reshape(owners, slot_rows), "cent", split_axis=0, concat_axis=0, tiled=True
        ),
        lax.all_to_all(
            totals.reshape(owners, slot_rows), "cent", split_axis=0, concat_axis=0, tiled=True
        ),
    )
    lookup = jnp.where(usable, route_code, 0)
    tile_norms = combine_norms(
        back_peaks.reshape(owners * capacity, tile_rows)[lookup],
        back_totals.reshape(owners * capacity, tile_rows)[lookup],
        usable,
    )
    slot_norms = jnp.dot(placing, tile_norms, precision=lax.Precision.HIGHEST)
    row_norms = lax.all_to_all(
        slot_norms.reshape(owners, slot_rows), "cent", split_axis=0, concat_axis=0, tiled=True
    ).reshape(-1)
    shares = jnp.where(occupied_rows[:, None], jnp.exp(logits - row_norms[:, None]), 0.0).astype(
        jnp.bfloat16
    )
    own_rows = centroids[0].astype(jnp.float32)
    own_count = own_rows.shape[0]
    block_mass = jnp.sum(shares, axis=0, dtype=jnp.float32)
    full_mass = lax.psum(block_mass, "dp")
    new_mass = lax.dynamic_slice_in_dim(full_mass, lax.axis_index("dp") * own_count, own_count, 0)
    block_sums = lax.dot_general(
        shares, incoming, (((0,), (0,)), ((), ())), preferred_element_type=jnp.float32
    )
    new_sums = lax.psum_scatter(block_sums, "dp", scatter_dimension=0, tiled=True)
    fresh = (new_sums + prior_weight * own_rows) / (new_mass[:, None] + prior_weight)
    return fresh[None]


def solution(mesh):
    in_specs = (
        P(("dp", "cent"), None),
        P(("dp", "cent"), None),
        P(("dp", "cent")),
        P("cent", "dp", None),
    )
    out_specs = P("cent", "dp", None)
    return jax.shard_map(
        per_device, mesh=mesh, in_specs=in_specs, out_specs=out_specs, check_vma=False
    )
```

profile of v0, /device:TPU:2, one launch (start us, length us, event | category | flops | bytes accessed | tf_op | source)
XLA Modules:
  0.0 253.5 jit_solution(3150392634497232480)
XLA Ops:
  6.5 0.7 all-gather.2.cloned.1.call-update
  7.3 0.7 iota_compare_fusion.1
  8.0 0.1 copy.53
  8.1 0.8 copy.56
  8.8 0.8 fusion.8
  9.6 0.1 copy.54
  9.9 0.1 eq.64
  10.1 0.1 copy.61
  10.2 0.7 gather_fusion.2
  11.1 0.2 fusion.2
  11.4 0.7 copy.66
  12.1 9.2 %all-to-all-start = ((bf16[16,2,3]{2,1,0:T(2,128)(2,1)}), bf16[16,2,3]{2,1,0:T(2,128)(2,1)S(1)}, u32[]{:S(2)}, u32[]{:S(2)}) async-start(bf16[16,2,3]{2,1,0:T(2,128)(2,1)} %bitcast.4), calls=%async_computation | async-start | bytes 16384 | tf_op jit(solution)/shard_map/all_to_all | solution.py:53
  21.3 0.2 reshape.117
  21.6 0.7 convolution_convert_fusion
  22.2 2.4 reshape.118
  24.6 2.8 %all-to-all-done = bf16[16,2,3]{2,1,0:T(2,128)(2,1)S(1)} async-done(((bf16[16,2,3]{2,1,0:T(2,128)(2,1)}), bf16[16,2,3]{2,1,0:T(2,128)(2,1)S(1)}, u32[]{:S(2)}, u32[]{:S(2)}) %all-to-all-start) | async-done | bytes 224 | tf_op jit(solution)/shard_map/all_to_all | solution.py:53
  27.5 5.0 %all-to-all-start.1 = ((bf16[16,64,1024]{2,1,0:T(8,128)(2,1)}), bf16[16,64,1024]{2,1,0:T(8,128)(2,1)S(1)}, u32[]{:S(2)}, u32[]{:S(2)}) async-start(bf16[16,64,1024]{2,1,0:T(8,128)(2,1)} %reshape.118), calls=%async_computation.1 | async-start | bytes 4194304 | tf_op jit(solution)/shard_map/all_to_all | solution.py:52
  32.6 0.1 copy.67
  32.7 24.7 %all-to-all-done.1 = bf16[16,64,1024]{2,1,0:T(8,128)(2,1)S(1)} async-done(((bf16[16,64,1024]{2,1,0:T(8,128)(2,1)}), bf16[16,64,1024]{2,1,0:T(8,128)(2,1)S(1)}, u32[]{:S(2)}, u32[]{:S(2)}) %all-to-all-start.1) | async-done | bytes 2097184 | tf_op jit(solution)/shard_map/all_to_all | solution.py:52
  57.4 28.3 %all-gather.2.cloned.1.call-done = bf16[1,1024,1024]{2,1,0:T(8,128)(2,1)} async-done(((bf16[1,32,1024]{2,1,0:T(8,128)(2,1)}), bf16[1,1024,1024]{2,1,0:T(8,128)(2,1)}) %all-gather.2.cloned.1.call-update) | async-done | bytes 2097168 | tf_op jit(solution)/shard_map/all_gather | solution.py:63
  85.7 5.9 %multiply_reduce_fusion = (f32[1024]{0:T(1024)S(1)}, f32[1024,1024]{0,1:T(8,128)}) fusion(bf16[1024,1024]{1,0:T(8,128)(2,1)S(1)} %bitcast.32, bf16[1,1024,1024]{2,1,0:T(8,128)(2,1)} %all-gather.2.cloned.1.call-done), kind=kOutput, calls=%fused_computation.7 | convolution fusion | flops 2149579776 | bytes 8392704 | tf_op jit(solution)/shard_map/dot_general | solution.py:61
  91.6 0.7 all_to_all.26
  92.3 7.3 %all-to-all-start.2 = ((f32[16,1,64]{2,1,0:T(1,128)}), f32[16,1,64]{2,1,0:T(1,128)S(1)}, u32[]{:S(2)}, u32[]{:S(2)}) async-start(f32[16,1,64]{2,1,0:T(1,128)} %all_to_all.26), calls=%async_computation.2 | async-start | bytes 16384 | tf_op jit(solution)/shard_map/all_to_all | solution.py:72
  99.6 2.9 %exponential_reduce_fusion = f32[1024]{0:T(1024)S(1)} fusion(f32[1024,1024]{0,1:T(8,128)} %get-tuple-element.8, f32[1024]{0:T(1024)S(1)} %get-tuple-element.7), kind=kLoop, calls=%fused_computation.6 | loop fusion | flops 3144704 | bytes 4202496 | tf_op jit(solution)/shard_map/reduce_sum | solution.py:70
  102.5 0.7 all_to_all.28
  103.2 2.5 all-to-all-done.2
  105.7 4.7 %all-to-all-start.3 = ((f32[16,1,64]{2,1,0:T(1,128)}), f32[16,1,64]{2,1,0:T(1,128)S(1)}, u32[]{:S(2)}, u32[]{:S(2)}) async-start(f32[16,1,64]{2,1,0:T(1,128)} %all_to_all.28), calls=%async_computation.3 | async-start | bytes 16384 | tf_op jit(solution)/shard_map/all_to_all | solution.py:75
  110.4 0.5 broadcast.138
  111.0 0.6 reduce.9
  111.7 0.6 gather_fusion
  112.3 0.1 select_reduce_fusion.1
  112.4 4.1 %all-to-all-done.3 = f32[16,1,64]{2,1,0:T(1,128)S(1)} async-done(((f32[16,1,64]{2,1,0:T(1,128)}), f32[16,1,64]{2,1,0:T(1,128)S(1)}, u32[]{:S(2)}, u32[]{:S(2)}) %all-to-all-start.3) | async-done | bytes 4128 | tf_op jit(solution)/shard_map/all_to_all | solution.py:75
  116.5 0.6 reduce.10
  117.2 0.6 gather_fusion.1
  117.8 0.1 select_reduce_fusion
  117.9 0.1 fusion.9
  118.0 0.7 all_to_all.30
  118.7 4.9 %all-to-all-start.4 = ((f32[16,1,64]{2,1,0:T(1,128)}), f32[16,1,64]{2,1,0:T(1,128)S(1)}, u32[]{:S(2)}, u32[]{:S(2)}) async-start(f32[16,1,64]{2,1,0:T(1,128)} %bitcast.9), calls=%async_computation.4 | async-start | bytes 16384 | tf_op jit(solution)/shard_map/all_to_all | solution.py:86
  123.6 0.1 copy.64
  123.7 0.1 broadcast_in_dim.66
  123.8 0.1 broadcast_in_dim.67
  123.9 5.8 %all-to-all-done.4 = f32[16,1,64]{2,1,0:T(1,128)S(1)} async-done(((f32[16,1,64]{2,1,0:T(1,128)}), f32[16,1,64]{2,1,0:T(1,128)S(1)}, u32[]{:S(2)}, u32[]{:S(2)}) %all-to-all-start.4) | async-done | bytes 4128 | tf_op jit(solution)/shard_map/all_to_all | solution.py:86
  129.8 0.6 reduce.11
  130.5 6.5 %fusion.5 = f32[1024,1024]{1,0:T(8,128)} fusion(bf16[1024,1024]{1,0:T(8,128)(2,1)S(1)} %bitcast.33, f32[1024,1024]{0,1:T(8,128)} %get-tuple-element.8, f32[1024]{0:T(1024)S(1)} %sub.44, pred[1024]{0:T(1024)(128)(4,1)S(1)} %broadcast_in_dim.67), kind=kOutput, calls=%fused_computation.15 | convolution fusion | flops 2151677952 | bytes 10490880 | tf_op jit(solution)/shard_map/dot_general | solution.py:97
  137.0 3.1 %convert_reduce_fusion = f32[1024]{0:T(1024)S(1)} fusion(f32[1024]{0:T(1024)S(1)} %sub.44, f32[1024,1024]{0,1:T(8,128)} %get-tuple-element.8, pred[1024]{0:T(1024)(128)(4,1)S(1)} %broadcast_in_dim.67), kind=kLoop, calls=%fused_computation.4 | loop fusion | flops 6290432 | bytes 4203520 | tf_op jit(solution)/shard_map/reduce_sum | solution.py:94
  140.1 45.8 %psum.7 = f32[1024]{0:T(1024)S(1)} all-reduce(f32[1024]{0:T(1024)S(1)} %convert_reduce_fusion), channel_id=1, replica_groups=mesh['dp'=32,'cent'=16] {'dp'}, use_global_device_ids=true, to_apply=%region_8.9 | all-reduce | flops 1024 | bytes 8192 | tf_op jit(solution)/shard_map/psum | solution.py:95
  186.0 59.1 %reduce-scatter.2.cloned.1.call-done = f32[32,1024]{1,0:T(8,128)} async-done(((f32[1024,1024]{1,0:T(8,128)}), f32[32,1024]{1,0:T(8,128)}) %reduce-scatter.2.cloned.1.call-update) | async-done | bytes 131088 | tf_op jit(solution)/shard_map/reduce_scatter | solution.py:100
  245.0 1.6 fusion.4
  (34 shorter events, 1.1 us)
Async XLA Ops:
  6.5 4.6 %copy-start.2 = (s32[8]{0:T(128)S(1)}, s32[8]{0:T(128)}, u32[]{:S(2)}) copy-start(s32[8]{0:T(128)} %param.6) | copy-start | bytes 100
  6.5 14.7 %copy-start = (bf16[256,1024]{1,0:T(8,128)(2,1)S(1)}, bf16[256,1024]{1,0:T(8,128)(2,1)}, u32[]{:S(2)}) copy-start(bf16[256,1024]{1,0:T(8,128)(2,1)} %param.4) | copy-start | bytes 1572868
  6.5 79.2 %all-gather.2.cloned.1.call-start = ((), (), s32[]{:S(2)}) async-start(), calls=%async_computation.6 | async-start | bytes 2162688 | tf_op jit(solution)/shard_map/all_gather | solution.py:63
  12.1 15.3 %all-to-all-start = ((bf16[16,2,3]{2,1,0:T(2,128)(2,1)}), bf16[16,2,3]{2,1,0:T(2,128)(2,1)S(1)}, u32[]{:S(2)}, u32[]{:S(2)}) async-start(bf16[16,2,3]{2,1,0:T(2,128)(2,1)} %bitcast.4), calls=%async_computation | async-start | bytes 16384 | tf_op jit(solution)/shard_map/all_to_all | solution.py:53
  27.5 29.9 %all-to-all-start.1 = ((bf16[16,64,1024]{2,1,0:T(8,128)(2,1)}), bf16[16,64,1024]{2,1,0:T(8,128)(2,1)S(1)}, u32[]{:S(2)}, u32[]{:S(2)}) async-start(bf16[16,64,1024]{2,1,0:T(8,128)(2,1)} %reshape.118), calls=%async_computation.1 | async-start | bytes 4194304 | tf_op jit(solution)/shard_map/all_to_all | solution.py:52
  92.3 13.4 %all-to-all-start.2 = ((f32[16,1,64]{2,1,0:T(1,128)}), f32[16,1,64]{2,1,0:T(1,128)S(1)}, u32[]{:S(2)}, u32[]{:S(2)}) async-start(f32[16,1,64]{2,1,0:T(1,128)} %all_to_all.26), calls=%async_computation.2 | async-start | bytes 16384 | tf_op jit(solution)/shard_map/all_to_all | solution.py:72
  105.7 10.8 %all-to-all-start.3 = ((f32[16,1,64]{2,1,0:T(1,128)}), f32[16,1,64]{2,1,0:T(1,128)S(1)}, u32[]{:S(2)}, u32[]{:S(2)}) async-start(f32[16,1,64]{2,1,0:T(1,128)} %all_to_all.28), calls=%async_computation.3 | async-start | bytes 16384 | tf_op jit(solution)/shard_map/all_to_all | solution.py:75
  118.7 11.0 %all-to-all-start.4 = ((f32[16,1,64]{2,1,0:T(1,128)}), f32[16,1,64]{2,1,0:T(1,128)S(1)}, u32[]{:S(2)}, u32[]{:S(2)}) async-start(f32[16,1,64]{2,1,0:T(1,128)} %bitcast.9), calls=%async_computation.4 | async-start | bytes 16384 | tf_op jit(solution)/shard_map/all_to_all | solution.py:86
  123.6 121.5 %reduce-scatter.2.cloned.1.call-start = ((), (), s32[]{:S(2)}) async-start(), calls=%async_computation.7 | async-start | bytes 4325376 | tf_op jit(solution)/shard_map/reduce_scatter | solution.py:100
  137.0 108.1 %copy-start.1 = (bf16[1,32,1024]{2,1,0:T(8,128)(2,1)S(1)}, bf16[1,32,1024]{2,1,0:T(8,128)(2,1)}, u32[]{:S(2)}) copy-start(bf16[1,32,1024]{2,1,0:T(8,128)(2,1)} %param.7) | copy-start | bytes 196612
Sparse Core Ops, SparseCore 0:
  9.5 76.2 all-gather.1
  137.1 107.8 reduce-scatter.1
where the time goes:
time: 254 us
  waiting for transfers between devices  128 us (50%)
  blocking collectives  45.8 us (18%)
  starting transfers between devices  31.1 us (12%)
  between operations  13.5 us (5%)
  matrix products  13.4 us (5%)
  other arithmetic  11.5 us (5%)
  local copies, waits for them, and re-layouts  9.97 us (4%)
    reduce_scatter x1, waiting for transfers between devices, per_device(): lax.psum_scatter(block_sums, 'dp', scatter_dimension=0, tiled=True)  59.1 us
    psum x1, blocking collectives, per_device(): full_mass = lax.psum(block_mass, 'dp')  45.8 us
    all_gather x1, waiting for transfers between devices, per_device(): lax.all_gather(centroids, 'dp', axis=1, tiled=True)[0]  28.3 us
    all_to_all x1, waiting for transfers between devices, per_device(): lax.all_to_all(outgoing, 'cent', split_axis=0, concat_axis=0, tiled=True)  24.7 us
    all_to_all x1, starting transfers between devices, per_device(): lax.all_to_all(slot_routes, 'cent', split_axis=0, concat_axis=0, tiled=True)  9.17 us
    all_to_all x1, starting transfers between devices, per_device(): lax.all_to_all(peaks.reshape(owners, slot_rows), 'cent', split_axis=0, co...  7.32 us
    dot_general x1, matrix products, per_device(): lax.dot_general(shares, incoming, (((0,), (0,)), ((), ())), preferred_ele...  6.49 us
    dot_general x1, matrix products, per_device(): lax.dot_general(incoming, lax.all_gather(centroids, 'dp', axis=1, tiled=T...  5.89 us
  transfers between devices with their start and end apart: 7, of which 7 were waited for; matrix products, arithmetic and copies ran while one was open for 7% of the time, Pallas kernels for 0%

commit v1 on v0

--- a/solution.py
+++ b/solution.py
@@ -60,7 +60,9 @@
     logits = (
         lax.dot_general(
             incoming,
-            lax.all_gather(centroids, "dp", axis=1, tiled=True)[0],
+            jnp.concatenate(
+                lax.all_to_all(jnp.stack([centroids] * lax.axis_size("dp")), "dp", 0, 0), axis=1
+            )[0],
             (((1,), (1,)), ((), ())),
             preferred_element_type=jnp.float32,
         )

time: 254 us -> 336 us (1.32)
  the two profiles are of different devices: /device:TPU:2 before, /device:TPU:4 now
where the time goes in v1:
time: 336 us; the launch traced here: 335 us
  waiting for transfers between devices  167 us (50%)
  blocking collectives  74.7 us (22%)
  starting transfers between devices  42.6 us (13%)
  between operations  13.6 us (4%)
  matrix products  13.4 us (4%)
  local copies, waits for them, and re-layouts  11.6 us (3%)
  other arithmetic  11.6 us (3%)
    all_to_all x1, waiting for transfers between devices, per_device(): lax.all_to_all(jnp.stack([centroids] * lax.axis_size('dp')), 'dp', 0, 0)  98.9 us
    reduce_scatter x1, waiting for transfers between devices, per_device(): lax.psum_scatter(block_sums, 'dp', scatter_dimension=0, tiled=True)  56.5 us
    psum x1, blocking collectives, per_device(): full_mass = lax.psum(block_mass, 'dp')  45.9 us
    all_to_all x1, blocking collectives, per_device(): lax.all_to_all(outgoing, 'cent', split_axis=0, concat_axis=0, tiled=True)  28.8 us
    all_to_all x1, starting transfers between devices, per_device(): lax.all_to_all(jnp.stack([centroids] * lax.axis_size('dp')), 'dp', 0, 0)  16.1 us
    all_to_all x1, starting transfers between devices, per_device(): lax.all_to_all(slot_routes, 'cent', split_axis=0, concat_axis=0, tiled=True)  9.15 us
  transfers between devices with their start and end apart: 6, of which 6 were waited for; matrix products, arithmetic and copies ran while one was open for 4% of the time, Pallas kernels for 0%

profile of v1, /device:TPU:4, one launch (start us, length us, event | category | flops | bytes accessed | tf_op | source)
XLA Modules:
  0.0 334.9 jit_solution(10831791050277216166)
XLA Ops:
  6.5 0.8 iota_compare_fusion.1
  7.3 0.1 copy.53
  7.4 0.8 copy.56
  8.2 0.8 fusion.4
  9.0 0.1 copy.54
  9.2 0.1 eq.64
  9.4 0.1 copy.61
  9.6 0.7 gather_fusion.2
  10.5 0.2 fusion
  10.7 0.7 copy.66
  11.5 9.1 %all-to-all-start = ((bf16[16,2,3]{2,1,0:T(2,128)(2,1)}), bf16[16,2,3]{2,1,0:T(2,128)(2,1)S(1)}, u32[]{:S(2)}, u32[]{:S(2)}) async-start(bf16[16,2,3]{2,1,0:T(2,128)(2,1)} %bitcast.4), calls=%async_computation | async-start | bytes 16384 | tf_op jit(solution)/shard_map/all_to_all | solution.py:53
  20.6 0.2 reshape.118
  20.9 0.7 convolution_convert_fusion
  21.6 2.4 reshape.119
  24.0 1.9 all-to-all-done
  25.9 28.8 %all_to_all.42 = bf16[16,64,1024]{2,1,0:T(8,128)(2,1)S(1)} all-to-all(bf16[16,64,1024]{2,1,0:T(8,128)(2,1)} %reshape.119), channel_id=1, replica_groups=mesh['dp'=32,'cent'=16] {'cent'}, dimensions={0} | all-to-all | bytes 4194304 | tf_op jit(solution)/shard_map/all_to_all | solution.py:52
  54.7 1.6 stack.2
  56.3 16.1 %all-to-all-start.2 = ((bf16[32,1,32,1024]{3,2,1,0:T(8,128)(2,1)}), bf16[32,1,32,1024]{3,2,1,0:T(8,128)(2,1)}, u32[]{:S(2)}, u32[]{:S(2)}) async-start(bf16[32,1,32,1024]{3,2,1,0:T(8,128)(2,1)} %stack.2), calls=%async_computation.2 | async-start | bytes 4194304 | tf_op jit(solution)/shard_map/all_to_all | solution.py:64
  72.6 0.1 copy.67
  72.7 98.9 %all-to-all-done.2 = bf16[32,1,32,1024]{3,2,1,0:T(8,128)(2,1)} async-done(((bf16[32,1,32,1024]{3,2,1,0:T(8,128)(2,1)}), bf16[32,1,32,1024]{3,2,1,0:T(8,128)(2,1)}, u32[]{:S(2)}, u32[]{:S(2)}) %all-to-all-start.2) | async-done | bytes 2097184 | tf_op jit(solution)/shard_map/all_to_all | solution.py:64
  171.7 5.9 %multiply_reduce_fusion = (f32[1024]{0:T(1024)S(1)}, f32[1024,1024]{0,1:T(8,128)}) fusion(bf16[1024,1024]{1,0:T(8,128)(2,1)S(1)} %bitcast.28, bf16[1024,1024]{1,0:T(8,128)(2,1)} %bitcast.9), kind=kOutput, calls=%fused_computation.7 | convolution fusion | flops 2149579776 | bytes 8392704 | tf_op jit(solution)/shard_map/dot_general | solution.py:61
  177.6 0.7 all_to_all.30
  178.2 6.1 %all-to-all-start.3 = ((f32[16,1,64]{2,1,0:T(1,128)}), f32[16,1,64]{2,1,0:T(1,128)S(1)}, u32[]{:S(2)}, u32[]{:S(2)}) async-start(f32[16,1,64]{2,1,0:T(1,128)} %all_to_all.30), calls=%async_computation.3 | async-start | bytes 16384 | tf_op jit(solution)/shard_map/all_to_all | solution.py:74
  184.4 2.9 exponential_reduce_fusion
  187.3 0.7 all_to_all.32
  188.0 1.7 all-to-all-done.3
  189.7 5.6 %all-to-all-start.4 = ((f32[16,1,64]{2,1,0:T(1,128)}), f32[16,1,64]{2,1,0:T(1,128)S(1)}, u32[]{:S(2)}, u32[]{:S(2)}) async-start(f32[16,1,64]{2,1,0:T(1,128)} %all_to_all.32), calls=%async_computation.4 | async-start | bytes 16384 | tf_op jit(solution)/shard_map/all_to_all | solution.py:77
  195.2 0.5 broadcast.141
  195.8 0.6 reduce.9
  196.5 0.6 gather_fusion
  197.1 0.1 select_reduce_fusion.1
  197.2 3.4 %all-to-all-done.4 = f32[16,1,64]{2,1,0:T(1,128)S(1)} async-done(((f32[16,1,64]{2,1,0:T(1,128)}), f32[16,1,64]{2,1,0:T(1,128)S(1)}, u32[]{:S(2)}, u32[]{:S(2)}) %all-to-all-start.4) | async-done | bytes 4128 | tf_op jit(solution)/shard_map/all_to_all | solution.py:77
  200.6 0.6 reduce.10
  201.3 0.6 gather_fusion.1
  201.9 0.1 select_reduce_fusion
  202.0 0.1 fusion.5
  202.1 0.7 all_to_all.34
  202.8 5.6 %all-to-all-start.5 = ((f32[16,1,64]{2,1,0:T(1,128)}), f32[16,1,64]{2,1,0:T(1,128)S(1)}, u32[]{:S(2)}, u32[]{:S(2)}) async-start(f32[16,1,64]{2,1,0:T(1,128)} %bitcast.10), calls=%async_computation.5 | async-start | bytes 16384 | tf_op jit(solution)/shard_map/all_to_all | solution.py:88
  208.4 0.1 copy.64
  208.5 0.1 broadcast_in_dim.66
  208.6 0.1 broadcast_in_dim.67
  208.7 5.0 %all-to-all-done.5 = f32[16,1,64]{2,1,0:T(1,128)S(1)} async-done(((f32[16,1,64]{2,1,0:T(1,128)}), f32[16,1,64]{2,1,0:T(1,128)S(1)}, u32[]{:S(2)}, u32[]{:S(2)}) %all-to-all-start.5) | async-done | bytes 4128 | tf_op jit(solution)/shard_map/all_to_all | solution.py:88
  213.7 0.6 reduce.11
  214.4 6.5 %fusion.1 = f32[1024,1024]{1,0:T(8,128)} fusion(bf16[1024,1024]{1,0:T(8,128)(2,1)S(1)} %bitcast.29, f32[1024,1024]{0,1:T(8,128)} %get-tuple-element.8, f32[1024]{0:T(1024)S(1)} %sub.44, pred[1024]{0:T(1024)(128)(4,1)S(1)} %broadcast_in_dim.67), kind=kOutput, calls=%fused_computation.11 | convolution fusion | flops 2151677952 | bytes 10490880 | tf_op jit(solution)/shard_map/dot_general | solution.py:99
  220.9 3.1 convert_reduce_fusion
  224.0 45.9 %psum.7 = f32[1024]{0:T(1024)S(1)} all-reduce(f32[1024]{0:T(1024)S(1)} %convert_reduce_fusion), channel_id=1, replica_groups=mesh['dp'=32,'cent'=16] {'dp'}, use_global_device_ids=true, to_apply=%region_8.9 | all-reduce | flops 1024 | bytes 8192 | tf_op jit(solution)/shard_map/psum | solution.py:97
  270.0 56.5 %reduce-scatter.2.cloned.1.call-done = f32[32,1024]{1,0:T(8,128)} async-done(((f32[1024,1024]{1,0:T(8,128)}), f32[32,1024]{1,0:T(8,128)}) %reduce-scatter.2.cloned.1.call-update) | async-done | bytes 131088 | tf_op jit(solution)/shard_map/reduce_scatter | solution.py:102
  326.4 1.6 divide_bitcast_fusion
  (33 shorter events, 1.1 us)
Async XLA Ops:
  6.5 4.0 %copy-start.2 = (s32[8]{0:T(128)S(1)}, s32[8]{0:T(128)}, u32[]{:S(2)}) copy-start(s32[8]{0:T(128)} %param.6) | copy-start | bytes 100
  6.5 14.1 %copy-start = (bf16[256,1024]{1,0:T(8,128)(2,1)S(1)}, bf16[256,1024]{1,0:T(8,128)(2,1)}, u32[]{:S(2)}) copy-start(bf16[256,1024]{1,0:T(8,128)(2,1)} %param.4) | copy-start | bytes 1572868
  11.5 14.4 %all-to-all-start = ((bf16[16,2,3]{2,1,0:T(2,128)(2,1)}), bf16[16,2,3]{2,1,0:T(2,128)(2,1)S(1)}, u32[]{:S(2)}, u32[]{:S(2)}) async-start(bf16[16,2,3]{2,1,0:T(2,128)(2,1)} %bitcast.4), calls=%async_computation | async-start | bytes 16384 | tf_op jit(solution)/shard_map/all_to_all | solution.py:53
  21.6 33.1 %copy-start.1 = (bf16[1,32,1024]{2,1,0:T(8,128)(2,1)S(1)}, bf16[1,32,1024]{2,1,0:T(8,128)(2,1)}, u32[]{:S(2)}) copy-start(bf16[1,32,1024]{2,1,0:T(8,128)(2,1)} %param.7) | copy-start | bytes 196612
  56.3 115.4 %all-to-all-start.2 = ((bf16[32,1,32,1024]{3,2,1,0:T(8,128)(2,1)}), bf16[32,1,32,1024]{3,2,1,0:T(8,128)(2,1)}, u32[]{:S(2)}, u32[]{:S(2)}) async-start(bf16[32,1,32,1024]{3,2,1,0:T(8,128)(2,1)} %stack.2), calls=%async_computation.2 | async-start | bytes 4194304 | tf_op jit(solution)/shard_map/all_to_all | solution.py:64
  178.2 11.4 %all-to-all-start.3 = ((f32[16,1,64]{2,1,0:T(1,128)}), f32[16,1,64]{2,1,0:T(1,128)S(1)}, u32[]{:S(2)}, u32[]{:S(2)}) async-start(f32[16,1,64]{2,1,0:T(1,128)} %all_to_all.30), calls=%async_computation.3 | async-start | bytes 16384 | tf_op jit(solution)/shard_map/all_to_all | solution.py:74
  189.7 10.9 %all-to-all-start.4 = ((f32[16,1,64]{2,1,0:T(1,128)}), f32[16,1,64]{2,1,0:T(1,128)S(1)}, u32[]{:S(2)}, u32[]{:S(2)}) async-start(f32[16,1,64]{2,1,0:T(1,128)} %all_to_all.32), calls=%async_computation.4 | async-start | bytes 16384 | tf_op jit(solution)/shard_map/all_to_all | solution.py:77
  202.8 10.9 %all-to-all-start.5 = ((f32[16,1,64]{2,1,0:T(1,128)}), f32[16,1,64]{2,1,0:T(1,128)S(1)}, u32[]{:S(2)}, u32[]{:S(2)}) async-start(f32[16,1,64]{2,1,0:T(1,128)} %bitcast.10), calls=%async_computation.5 | async-start | bytes 16384 | tf_op jit(solution)/shard_map/all_to_all | solution.py:88
  208.4 118.1 %reduce-scatter.2.cloned.1.call-start = ((), (), s32[]{:S(2)}) async-start(), calls=%async_computation.7 | async-start | bytes 4325376 | tf_op jit(solution)/shard_map/reduce_scatter | solution.py:102
Sparse Core Ops, SparseCore 0:
  221.0 105.3 reduce-scatter.1
